TPU v7x, 256 devices: a whole 4x4x8 slice. The times are simulated.
256 devices in a mesh: req: 32 (over x, z), mlp: 8 (over y, core).
Axes of the slice: x: 4, y: 4, z: 8, core: 2. Of those that a mesh axis runs over, the one named last changes fastest.
Arguments:
- x_pages: bfloat16 [1024, 8, 4096], P('req', None, 'mlp'), may hold values from -6 to 6
- page_owner: int32 [1024], P('req'), may hold values from 0 to 31, as said below
- request_id: int32 [8192], P('req'), may hold values from 0 to 8191, as said below
- adapter_table: int32 [8192], P('req'), may hold values from 0 to 63
- ln_gain: float32 [4096], replicated, may hold values from 0.5 to 1.5
- ln_bias: float32 [4096], replicated, may hold values from -3 to 3
- w_query: bfloat16 [4096, 2048], P('req', 'mlp'), may hold values from -0.09375 to 0.09375
- w_key: bfloat16 [4096, 2048], P('req', 'mlp'), may hold values from -0.09375 to 0.09375
- w_value: bfloat16 [4096, 2048], P('req', 'mlp'), may hold values from -0.09375 to 0.09375
- w_attn_out: bfloat16 [2048, 4096], P('mlp', 'req'), may hold values from -0.125 to 0.125
- down_query: bfloat16 [4096, 1024], P('mlp'), may hold values from -0.09375 to 0.09375
- up_query: bfloat16 [1024, 2048], P(None, 'mlp'), may hold values from -1.5 to 1.5
- down_value: bfloat16 [4096, 1024], P('mlp'), may hold values from -0.09375 to 0.09375
- up_value: bfloat16 [1024, 2048], P(None, 'mlp'), may hold values from -1.5 to 1.5
- w_fc_in: bfloat16 [4096, 8192], P('req', 'mlp'), may hold values from -0.09375 to 0.09375
- b_fc_in: float32 [8192], P('mlp'), may hold values from -3 to 3
- down_fc: bfloat16 [4096, 1024], P('mlp'), may hold values from -0.09375 to 0.09375
- up_fc: bfloat16 [1024, 8192], P(None, 'mlp'), may hold values from -1.5 to 1.5
- w_fc_out: bfloat16 [8192, 4096], P('mlp', 'req'), may hold values from -0.0625 to 0.0625
- b_fc_out: float32 [4096], P('mlp'), may hold values from -3 to 3
Outputs:
- out_pages: bfloat16 [1024, 8, 4096], P('req', None, 'mlp')
Inputs may be any that keep to these rules, and one draw needn't show every extreme that they name: `page_owner`: every owner receives exactly 32 pages, at most 2 of them from one device, and some device sends exactly 2 pages to some owner. `request_id`: ids never fall; every request lies inside one owner's block of 256 rows, and the ids of block k lie in k * 256 to k * 256 + 255; some request is 256 long.
All inputs are finite; a program needn't handle non-finite values.
Results may differ from a plain program's by a relative error of at most 0.006.
Values may be sent and summed in bfloat16 or wider, within the bound.
No kernel may reach another device: no remote copies, remote signals or barrier semaphores. Data moves between devices by JAX's collectives and lax.ppermute only.
A program may use at most 128 MiB of HBM per device.

v0:
```python
import jax
import jax.numpy as jnp
from jax import lax
from jax.sharding import PartitionSpec as P

HS = 256
ROT = 64
NAD = 64
R = 16
EPS = 1e-05


def gelu_tanh(v):
    return 0.5 * v * (1.0 + jnp.tanh(0.7978845608028654 * (v + 0.044715 * v * v * v)))


def rotate(block, pos):
    half = ROT // 2
    freq = jnp.power(10000.0, -jnp.arange(half).astype(jnp.float32) * 2.0 / ROT)
    angle = pos.astype(jnp.float32)[:, None, None] * freq[None, None, :]
    cosine = jnp.cos(angle)
    sine = jnp.sin(angle)
    even = block[:, :, 0:ROT:2]
    odd = block[:, :, 1:ROT:2]
    turned = jnp.stack([even * cosine - odd * sine, odd * cosine + even * sine], axis=-1)
    turned = turned.reshape(block.shape[0], block.shape[1], ROT)
    return jnp.concatenate([turned, block[:, :, ROT:]], axis=2)


def on_device(
    x_pages,
    page_owner,
    request_id,
    adapter_table,
    ln_gain,
    ln_bias,
    w_query,
    w_key,
    w_value,
    w_attn_out,
    down_query,
    up_query,
    down_value,
    up_value,
    w_fc_in,
    b_fc_in,
    down_fc,
    up_fc,
    w_fc_out,
    b_fc_out,
):
    groups = lax.axis_size("req")
    pg_dev = x_pages.shape[0]
    page_len = x_pages.shape[1]
    width_m = x_pages.shape[2]
    tok = request_id.shape[0]
    per_owner = pg_dev // groups + 1
    slots = groups * per_owner
    page_iota = jnp.arange(pg_dev)
    earlier = (page_owner[None, :] == page_owner[:, None]) & (
        page_iota[None, :] < page_iota[:, None]
    )
    rank = jnp.sum(earlier.astype(jnp.int32), axis=1)
    slot = page_owner * per_owner + rank
    place = (slot[None, :] == jnp.arange(slots)[:, None]).astype(jnp.bfloat16)
    flat_pages = x_pages.reshape(pg_dev, page_len * width_m)
    outgoing = jnp.dot(place, flat_pages, preferred_element_type=jnp.float32).astype(jnp.bfloat16)
    outgoing = outgoing.reshape(groups, per_owner, page_len * width_m)
    filled = jnp.sum(place, axis=1).reshape(groups, per_owner)
    arrived, marks = (
        lax.all_to_all(outgoing, "req", split_axis=0, concat_axis=0, tiled=True),
        lax.all_to_all(filled, "req", split_axis=0, concat_axis=0, tiled=True),
    )
    valid = marks.reshape(slots).astype(jnp.float32)
    position = jnp.cumsum(valid) - 1.0
    take = (
        (position[None, :] == jnp.arange(pg_dev).astype(jnp.float32)[:, None])
        & (valid[None, :] > 0.5)
    ).astype(jnp.bfloat16)
    own_x = jnp.dot(
        take, arrived.reshape(slots, page_len * width_m), preferred_element_type=jnp.float32
    )
    own_x = own_x.astype(jnp.bfloat16).reshape(tok, width_m)
    column = lax.axis_index("mlp") * width_m
    whole = lax.all_gather(own_x, "mlp", axis=1, tiled=True).astype(jnp.float32)
    mean = jnp.mean(whole, axis=1, keepdims=True)
    var = jnp.mean(jnp.square(whole - mean), axis=1, keepdims=True)
    full_ln = ((whole - mean) * lax.rsqrt(var + EPS) * ln_gain + ln_bias).astype(jnp.bfloat16)
    ln_m = lax.dynamic_slice_in_dim(full_ln, column, width_m, 1)
    local_req = request_id - lax.axis_index("req") * tok
    lookup = local_req[:, None] == jnp.arange(tok)[None, :]
    adapter = jnp.sum(jnp.where(lookup, adapter_table[None, :], 0), axis=1)
    onehot = (adapter[:, None] == jnp.arange(NAD)[None, :]).astype(jnp.float32)
    onehot_low = onehot.astype(jnp.bfloat16)

    def pick(down):
        spread = jnp.dot(ln_m, down, preferred_element_type=jnp.float32).reshape(tok, NAD, R)
        return jnp.sum(spread * onehot[:, :, None], axis=1)

    picked = lax.psum((pick(down_query), pick(down_value), pick(down_fc)), "mlp")

    def lift(chosen, up):
        expanded = (onehot_low[:, :, None] * chosen.astype(jnp.bfloat16)[:, None, :]).reshape(
            tok, NAD * R
        )
        return jnp.dot(expanded, up, preferred_element_type=jnp.float32)

    row_iota = jnp.arange(tok)
    start = jnp.sum((request_id[None, :] < request_id[:, None]).astype(jnp.int32), axis=1)
    pos = row_iota - start
    mask = (request_id[:, None] == request_id[None, :]) & (row_iota[None, :] <= row_iota[:, None])
    heads_w = w_query.shape[1]
    pieces = (
        lax.all_gather(w_query, "req", axis=0, tiled=True),
        lax.all_gather(w_key, "req", axis=0, tiled=True),
        lax.all_gather(w_value, "req", axis=0, tiled=True),
    )
    cols = full_ln
    base_q, base_k, base_v = tuple(
        [jnp.dot(cols, piece, preferred_element_type=jnp.float32) for piece in pieces]
    )
    query = rotate(
        (base_q + lift(picked[0], up_query)).reshape(tok, heads_w // HS, HS), pos
    ).astype(jnp.bfloat16)
    keys = rotate(base_k.reshape(tok, heads_w // HS, HS), pos).astype(jnp.bfloat16)
    value = (
        (base_v + lift(picked[1], up_value)).astype(jnp.bfloat16).reshape(tok, heads_w // HS, HS)
    )
    scores = jnp.einsum("qhd,khd->hqk", query, keys, preferred_element_type=jnp.float32) * HS ** (
        -0.5
    )
    scores = jnp.where(mask[None, :, :], scores, -1e30)
    top = jnp.max(scores, axis=2, keepdims=True)
    weights = jnp.exp(scores - top)
    probs = (weights / jnp.sum(weights, axis=2, keepdims=True)).astype(jnp.bfloat16)
    mixed_heads = jnp.einsum("hqk,khd->qhd", probs, value, preferred_element_type=jnp.float32)
    attn = mixed_heads.astype(jnp.bfloat16).reshape(tok, heads_w)
    cols = full_ln
    hidden_pre = jnp.dot(
        cols, lax.all_gather(w_fc_in, "req", axis=0, tiled=True), preferred_element_type=jnp.float32
    )
    hidden_pre = hidden_pre + lift(picked[2], up_fc) + b_fc_in
    hidden = gelu_tanh(hidden_pre).astype(jnp.bfloat16)
    pieces = (
        lax.all_gather(w_attn_out, "req", axis=1, tiled=True),
        lax.all_gather(w_fc_out, "req", axis=1, tiled=True),
    )
    part = jnp.dot(attn, pieces[0], preferred_element_type=jnp.float32) + jnp.dot(
        hidden, pieces[1], preferred_element_type=jnp.float32
    )
    shares = lax.psum_scatter(part, "mlp", scatter_dimension=1, tiled=True)
    result = (own_x.astype(jnp.float32) + shares + b_fc_out).astype(jnp.bfloat16)
    back_flat = result.reshape(pg_dev, page_len * width_m)
    leaving = jnp.dot(take.T, back_flat, preferred_element_type=jnp.float32).astype(jnp.bfloat16)
    leaving = leaving.reshape(groups, per_owner, page_len * width_m)
    returned = lax.all_to_all(leaving, "req", split_axis=0, concat_axis=0, tiled=True)
    pages_back = jnp.dot(
        place.T, returned.reshape(slots, page_len * width_m), preferred_element_type=jnp.float32
    )
    return pages_back.astype(jnp.bfloat16).reshape(pg_dev, page_len, width_m)


def solution(mesh):
    in_specs = (
        P("req", None, "mlp"),
        P("req"),
        P("req"),
        P("req"),
        P(),
        P(),
        P("req", "mlp"),
        P("req", "mlp"),
        P("req", "mlp"),
        P("mlp", "req"),
        P("mlp", None),
        P(None, "mlp"),
        P("mlp", None),
        P(None, "mlp"),
        P("req", "mlp"),
        P("mlp"),
        P("mlp", None),
        P(None, "mlp"),
        P("mlp", "req"),
        P("mlp"),
    )
    out_specs = P("req", None, "mlp")
    return jax.shard_map(
        on_device, mesh=mesh, in_specs=in_specs, out_specs=out_specs, check_vma=False
    )
```

profile of v0, /device:TPU:57, one launch (start us, length us, event | category | flops | bytes accessed | tf_op | source)
XLA Modules:
  0.0 669.1 jit_solution(17255531953203514862)
XLA Ops:
  6.5 1.0 convert_reduce_fusion.3
  7.5 0.7 multiply_add_fusion.1
  8.3 0.7 all_to_all.16
  9.0 10.6 %all-to-all-start = ((bf16[32,1,2]{2,1,0:T(2,128)(2,1)}), bf16[32,1,2]{2,1,0:T(2,128)(2,1)S(1)}, u32[]{:S(2)}, u32[]{:S(2)}) async-start(bf16[32,1,2]{2,1,0:T(2,128)(2,1)} %all_to_all.16), calls=%async_computation | async-start | bytes 32768 | tf_op jit(solution)/shard_map/all_to_all | solution.py:72
  19.7 1.0 copy.46
  21.1 1.1 reshape.339
  22.3 5.1 all-to-all-done
  27.4 4.7 all-to-all-start.1
  32.6 14.9 %all-to-all-done.1 = bf16[32,2,4096]{2,1,0:T(2,128)(2,1)S(1)} async-done(((bf16[32,2,4096]{2,1,0:T(2,128)(2,1)}), bf16[32,2,4096]{2,1,0:T(2,128)(2,1)S(1)}, u32[]{:S(2)}, u32[]{:S(2)}) %all-to-all-start.1) | async-done | bytes 524320 | tf_op jit(solution)/shard_map/all_to_all | solution.py:71
  48.1 0.8 reshape.341
  49.0 0.7 all-gather.12.cloned.1.call-update
  49.7 0.7 all-gather.14.cloned.1.call-update
  50.4 0.5 all-gather.10.cloned.1.call-update
  51.0 0.5 all-gather.18.cloned.1.call-update
  51.6 0.5 all-gather.20.cloned.1.call-update
  52.2 0.7 all-gather.16.cloned.1.call-update
  52.9 0.5 multiply_power_fusion
  53.8 21.0 %all-gather.8.cloned.1.call-done = bf16[256,4096]{1,0:T(8,128)(2,1)} async-done(((bf16[256,512]{1,0:T(8,128)(2,1)}), bf16[256,4096]{1,0:T(8,128)(2,1)}) %all-gather.8.cloned.1.call-update) | async-done | bytes 2097168 | tf_op jit(solution)/shard_map/all_gather | solution.py:85
  74.8 2.1 convert_reduce_fusion
  77.1 0.7 fusion.2
  77.8 1.0 fusion.5
  79.0 0.6 fusion.28
  79.6 1.4 copy-done.5
  81.0 0.6 fusion.24
  81.6 0.6 fusion.26
  82.2 0.4 multiply_reduce_fusion.1
  82.6 24.0 %all-reduce = (bf16[256,16]{0,1:T(8,128)(2,1)S(1)}, bf16[256,16]{0,1:T(8,128)(2,1)S(1)}, bf16[256,16]{0,1:T(8,128)(2,1)S(1)}) all-reduce(f32[256,16]{0,1:T(8,128)S(1)} %get-tuple-element.6, f32[256,16]{0,1:T(8,128)S(1)} %get-tuple-element.7, f32[256,16]{0,1:T(8,128)S(1)} %get-tuple-element.5), channel_id=1, replica_groups=mesh['req'=32,'mlp'=8] {'mlp'}, use_global_device_ids=true, to_apply=%region_14.15 | all-reduce | flops 12288 | bytes 73728 | tf_op jit(solution)/shard_map/psum | solution.py:100
  106.6 44.5 %all-gather.12.cloned.1.call-done = bf16[4096,256]{1,0:T(8,128)(2,1)} async-done(((bf16[128,256]{1,0:T(8,128)(2,1)}), bf16[4096,256]{1,0:T(8,128)(2,1)}) %all-gather.12.cloned.1.call-update) | async-done | bytes 2097168 | tf_op jit(solution)/shard_map/all_gather | solution.py:114
  151.1 3.2 fusion.85
  154.9 0.7 copy-done.7
  155.5 73.3 %all-gather.14.cloned.1.call-done = bf16[4096,256]{1,0:T(8,128)(2,1)} async-done(((bf16[128,256]{1,0:T(8,128)(2,1)}), bf16[4096,256]{1,0:T(8,128)(2,1)}) %all-gather.14.cloned.1.call-update) | async-done | bytes 2097168 | tf_op jit(solution)/shard_map/all_gather | solution.py:115
  228.8 3.1 convolution_bitcast_fusion
  232.0 0.8 fusion.61
  233.0 0.9 fusion.40
  234.3 72.1 %all-gather.10.cloned.1.call-done = bf16[4096,256]{1,0:T(8,128)(2,1)} async-done(((bf16[128,256]{1,0:T(8,128)(2,1)}), bf16[4096,256]{1,0:T(8,128)(2,1)}) %all-gather.10.cloned.1.call-update) | async-done | bytes 2097168 | tf_op jit(solution)/shard_map/all_gather | solution.py:116
  306.4 3.0 fusion.84
  309.8 97.4 %all-gather.18.cloned.1.call-done = bf16[4096,1024]{1,0:T(8,128)(2,1)} async-done(((bf16[128,1024]{1,0:T(8,128)(2,1)}), bf16[4096,1024]{1,0:T(8,128)(2,1)}) %all-gather.18.cloned.1.call-update) | async-done | bytes 8388624 | tf_op jit(solution)/shard_map/all_gather | solution.py:140
  407.2 7.3 %fusion.86 = f32[256,1024]{1,0:T(8,128)} fusion(bf16[256,4096]{1,0:T(8,128)(2,1)} %copy-done.1, bf16[4096,1024]{1,0:T(8,128)(2,1)} %all-gather.18.cloned.1.call-done), kind=kOutput, calls=%fused_computation.132 | convolution fusion | flops 2147483648 | bytes 11534336 | tf_op jit(solution)/shard_map/dot_general | solution.py:139
  414.5 92.1 %all-gather.20.cloned.1.call-done = bf16[1024,4096]{1,0:T(8,128)(2,1)} async-done(((bf16[1024,128]{1,0:T(8,128)(2,1)}), bf16[1024,4096]{1,0:T(8,128)(2,1)}) %all-gather.20.cloned.1.call-update) | async-done | bytes 8388624 | tf_op jit(solution)/shard_map/all_gather | solution.py:146
  506.6 8.9 %fusion.16 = f32[256,4096]{1,0:T(8,128)} fusion(bf16[1024,4096]{1,0:T(8,128)(2,1)} %all-gather.20.cloned.1.call-done, f32[256,1024]{1,0:T(8,128)} %fusion.86, bf16[256,1024]{0,1:T(8,128)(2,1)S(1)} %bitcast.65, bf16[1024,1024]{1,0:T(8,128)(2,1)S(1)} %copy-done, f32[1024]{0:T(1024)S(1)} %copy-done.12), kind=kOutput, calls=%fused_computation.33 | convolution fusion | flops 2687238144 | bytes 16257024 | tf_op jit(solution)/shard_map/dot_general | solution.py:148
  515.5 67.1 %all-gather.16.cloned.1.call-done = bf16[256,4096]{1,0:T(8,128)(2,1)} async-done(((bf16[256,128]{1,0:T(8,128)(2,1)}), bf16[256,4096]{1,0:T(8,128)(2,1)}) %all-gather.16.cloned.1.call-update) | async-done | bytes 2097168 | tf_op jit(solution)/shard_map/all_gather | solution.py:145
  582.6 5.7 convolution_add_fusion
  588.3 42.6 %reduce-scatter.2.cloned.1.call-done = f32[256,512]{1,0:T(8,128)} async-done(((f32[256,4096]{1,0:T(8,128)}), f32[256,512]{1,0:T(8,128)}) %reduce-scatter.2.cloned.1.call-update) | async-done | bytes 524304 | tf_op jit(solution)/shard_map/reduce_scatter | solution.py:151
  630.9 1.1 add_convert_fusion
  632.2 0.4 convolution_convert_fusion
  632.9 27.0 %all_to_all.20 = bf16[32,2,4096]{2,1,0:T(2,128)(2,1)} all-to-all(bf16[32,2,4096]{2,1,0:T(2,128)(2,1)S(1)} %reshape.349), channel_id=1, replica_groups=mesh['req'=32,'mlp'=8] {'req'}, dimensions={0} | all-to-all | bytes 1048576 | tf_op jit(solution)/shard_map/all_to_all | solution.py:156
  660.0 1.2 reshape.350
  661.5 0.8 copy.47
  (84 shorter events, 4.6 us)
Async XLA Ops:
  6.5 500.1 %copy-start = (bf16[1024,1024]{1,0:T(8,128)(2,1)S(1)}, bf16[1024,1024]{1,0:T(8,128)(2,1)}, u32[]{:S(2)}) copy-start(bf16[1024,1024]{1,0:T(8,128)(2,1)} %param.37) | copy-start | bytes 6291460
  8.2 23.9 %copy-start.15 = (s32[32]{0:T(128)}, s32[32]{0:T(128)S(1)}, u32[]{:S(2)}) copy-start(s32[32]{0:T(128)S(1)} %multiply_add_fusion.1) | copy-start | bytes 388
  9.0 18.3 %all-to-all-start = ((bf16[32,1,2]{2,1,0:T(2,128)(2,1)}), bf16[32,1,2]{2,1,0:T(2,128)(2,1)S(1)}, u32[]{:S(2)}, u32[]{:S(2)}) async-start(bf16[32,1,2]{2,1,0:T(2,128)(2,1)} %all_to_all.16), calls=%async_computation | async-start | bytes 32768 | tf_op jit(solution)/shard_map/all_to_all | solution.py:72
  22.3 31.2 %copy-start.13 = (s32[256]{0:T(256)S(1)}, s32[256]{0:T(256)}, u32[]{:S(2)}) copy-start(s32[256]{0:T(256)} %param.22) | copy-start | bytes 3076
  22.3 31.4 %copy-start.19 = (s32[256]{0:T(256)S(1)}, s32[256]{0:T(256)}, u32[]{:S(2)}) copy-start(s32[256]{0:T(256)} %param.23) | copy-start | bytes 3076
  27.4 20.2 %all-to-all-start.1 = ((bf16[32,2,4096]{2,1,0:T(2,128)(2,1)}), bf16[32,2,4096]{2,1,0:T(2,128)(2,1)S(1)}, u32[]{:S(2)}, u32[]{:S(2)}) async-start(bf16[32,2,4096]{2,1,0:T(2,128)(2,1)} %reshape.339), calls=%async_computation.1 | async-start | bytes 1048576 | tf_op jit(solution)/shard_map/all_to_all | solution.py:71
  32.0 42.8 %all-gather.8.cloned.1.call-start = ((), (), s32[]{:S(2)}) async-start(), calls=%async_computation.4 | async-start | bytes 2359296 | tf_op jit(solution)/shard_map/all_gather | solution.py:85
  32.1 21.5 %copy-start.17 = (f32[32]{0:T(128)}, f32[32]{0:T(128)S(1)}, u32[]{:S(2)}) copy-start(f32[32]{0:T(128)S(1)} %iota_convert_fusion) | copy-start | bytes 388
  48.9 102.2 %all-gather.12.cloned.1.call-start = ((), (), s32[]{:S(2)}) async-start(), calls=%async_computation.6 | async-start | bytes 2162688 | tf_op jit(solution)/shard_map/all_gather | solution.py:114
  49.7 179.2 %all-gather.14.cloned.1.call-start = ((), (), s32[]{:S(2)}) async-start(), calls=%async_computation.7 | async-start | bytes 2162688 | tf_op jit(solution)/shard_map/all_gather | solution.py:115
  50.4 256.0 %all-gather.10.cloned.1.call-start = ((), (), s32[]{:S(2)}) async-start(), calls=%async_computation.5 | async-start | bytes 2162688 | tf_op jit(solution)/shard_map/all_gather | solution.py:116
  51.0 356.2 %all-gather.18.cloned.1.call-start = ((), (), s32[]{:S(2)}) async-start(), calls=%async_computation.9 | async-start | bytes 8650752 | tf_op jit(solution)/shard_map/all_gather | solution.py:140
  51.6 455.1 %all-gather.20.cloned.1.call-start = ((), (), s32[]{:S(2)}) async-start(), calls=%async_computation.10 | async-start | bytes 8650752 | tf_op jit(solution)/shard_map/all_gather | solution.py:146
  52.1 530.4 %all-gather.16.cloned.1.call-start = ((), (), s32[]{:S(2)}) async-start(), calls=%async_computation.8 | async-start | bytes 2162688 | tf_op jit(solution)/shard_map/all_gather | solution.py:145
  52.9 578.0 %reduce-scatter.2.cloned.1.call-start = ((), (), s32[]{:S(2)}) async-start(), calls=%async_computation.11 | async-start | bytes 4718592 | tf_op jit(solution)/shard_map/reduce_scatter | solution.py:151
  74.8 2.2 copy-start.2
  74.8 2.9 copy-start.10
  74.8 2.9 copy-start.11
  77.8 1.2 copy-start.4
  79.0 2.6 copy-start.1
  79.0 2.0 copy-start.5
  79.0 2.6 copy-start.6
  151.1 3.3 copy-start.8
  154.8 0.7 copy-start.7
  306.4 3.0 copy-start.9
  309.8 196.8 %copy-start.12 = (f32[1024]{0:T(1024)S(1)}, f32[1024]{0:T(1024)}, u32[]{:S(2)}) copy-start(f32[1024]{0:T(1024)} %param.35) | copy-start | bytes 12292
  588.3 42.6 %copy-start.3 = (bf16[256,512]{1,0:T(8,128)(2,1)S(1)}, bf16[256,512]{1,0:T(8,128)(2,1)}, u32[]{:S(2)}) copy-start(bf16[256,512]{1,0:T(8,128)(2,1)} %reshape.341) | copy-start | bytes 786436
  588.3 42.6 %copy-start.14 = (f32[512]{0:T(512)S(1)}, f32[512]{0:T(512)}, u32[]{:S(2)}) copy-start(f32[512]{0:T(512)} %param.39) | copy-start | bytes 6148
  588.3 43.9 %copy-start.18 = (f32[32]{0:T(128)S(1)}, f32[32]{0:T(128)}, u32[]{:S(2)}) copy-start(f32[32]{0:T(128)} %copy-done.17) | copy-start | bytes 388
  632.2 29.1 %copy-start.16 = (s32[32]{0:T(128)S(1)}, s32[32]{0:T(128)}, u32[]{:S(2)}) copy-start(s32[32]{0:T(128)} %copy-done.15) | copy-start | bytes 388
Sparse Core Ops, SparseCore 0:
  49.0 25.7 all-gather.7
  77.4 73.6 all-gather.11
  153.7 75.0 all-gather.13
  231.3 75.0 all-gather.9
  308.9 98.2 all-gather.17
  409.5 97.0 all-gather.19
  509.1 73.4 all-gather.15
  588.4 42.4 reduce-scatter.1
where the time goes:
time: 670 us; the launch traced here: 669 us
  waiting for transfers between devices  534 us (80%)
  blocking collectives  51 us (8%)
  matrix products  35.3 us (5%)
  starting transfers between devices  15.6 us (2%)
  between operations  13.9 us (2%)
  local copies, waits for them, and re-layouts  10.2 us (2%)
  other arithmetic  9.33 us (1%)
    all_gather x1, waiting for transfers between devices, on_device(): lax.all_gather(w_fc_in, 'req', axis=0, tiled=True)  97.4 us
    all_gather x1, waiting for transfers between devices, on_device(): lax.all_gather(w_fc_out, 'req', axis=1, tiled=True)  92.1 us
    all_gather x1, waiting for transfers between devices, on_device(): lax.all_gather(w_key, 'req', axis=0, tiled=True)  73.3 us
    all_gather x1, waiting for transfers between devices, on_device(): lax.all_gather(w_value, 'req', axis=0, tiled=True)  72.1 us
    all_gather x1, waiting for transfers between devices, on_device(): lax.all_gather(w_attn_out, 'req', axis=1, tiled=True)  67.1 us
    all_gather x1, waiting for transfers between devices, on_device(): lax.all_gather(w_query, 'req', axis=0, tiled=True)  44.5 us
    reduce_scatter x1, waiting for transfers between devices, on_device(): shares = lax.psum_scatter(part, 'mlp', scatter_dimension=1, tiled=True)  42.6 us
    all_to_all x1, blocking collectives, on_device(): lax.all_to_all(leaving, 'req', split_axis=0, concat_axis=0, tiled=True)  27 us
  transfers between devices with their start and end apart: 10, of which 10 were waited for; matrix products, arithmetic and copies ran while one was open for 6% of the time, Pallas kernels for 0%

commit v1 on v0

--- a/solution.py
+++ b/solution.py
@@ -1,3 +1,4 @@
+import functools
 import jax
 import jax.numpy as jnp
 from jax import lax
@@ -8,6 +9,32 @@
 NAD = 64
 R = 16
 EPS = 1e-05
+
+
+def numbers_pass(s0, ndim_at):
+    piece_now = lax.axis_size("mlp")
+    newest = lax.axis_index("mlp")
+    mid_arr, reply, plain = (piece_now, newest, s0.shape[ndim_at])
+    kept_rows = [(dev_i, (dev_i + 1) % mid_arr) for dev_i in range(mid_arr)]
+    windows = [(dev_i, (dev_i - 1) % mid_arr) for dev_i in range(mid_arr)]
+    all_rows = jnp.zeros((*s0.shape[:ndim_at], mid_arr * plain, *s0.shape[ndim_at + 1 :]), s0.dtype)
+    all_rows = lax.dynamic_update_slice_in_dim(all_rows, s0, reply * plain, axis=ndim_at)
+    seen_now = tile_out = s0
+    placed = mid_arr // 2
+    for to_i in [*range(1, placed + 1)]:
+        seen_now = lax.ppermute(seen_now, axis_name="mlp", perm=kept_rows)
+        all_rows = lax.dynamic_update_slice_in_dim(
+            all_rows, seen_now, (reply - to_i) % mid_arr * plain, axis=ndim_at
+        )
+        if to_i < mid_arr - placed:
+            tile_out = lax.ppermute(tile_out, axis_name="mlp", perm=windows)
+            all_rows = lax.dynamic_update_slice_in_dim(
+                all_rows, tile_out, (reply + to_i) % mid_arr * plain, axis=ndim_at
+            )
+    return all_rows
+
+
+check_field = functools.partial(numbers_pass, ndim_at=1)
 
 
 def gelu_tanh(v):
@@ -82,7 +109,7 @@
     )
     own_x = own_x.astype(jnp.bfloat16).reshape(tok, width_m)
     column = lax.axis_index("mlp") * width_m
-    whole = lax.all_gather(own_x, "mlp", axis=1, tiled=True).astype(jnp.float32)
+    whole = check_field(own_x).astype(jnp.float32)
     mean = jnp.mean(whole, axis=1, keepdims=True)
     var = jnp.mean(jnp.square(whole - mean), axis=1, keepdims=True)
     full_ln = ((whole - mean) * lax.rsqrt(var + EPS) * ln_gain + ln_bias).astype(jnp.bfloat16)

time: 670 us -> 604 us (0.901)
  waiting for transfers between devices: 534 us -> 450 us
  starting transfers between devices: 15.6 us -> 29.6 us
    all_gather x1, waiting for transfers between devices: 44.5 us -> 0.02 us  [on_device(): lax.all_gather(w_query, 'req', axis=0, tiled=True)]
    all_gather x1, waiting for transfers between devices: 73.3 us -> 42.9 us  [on_device(): lax.all_gather(w_key, 'req', axis=0, tiled=True)]
    all_gather x1 -> x0, waiting for transfers between devices: 21 us -> none  [on_device(): whole = lax.all_gather(own_x, 'mlp', axis=1, tiled=True).astype(jnp.float32)]
    ppermute x0 -> x7, starting transfers between devices: none -> 14.1 us  [the longest x4 14 us: numbers_pass(): seen_now = lax.ppermute(seen_now, axis_name='mlp', perm=kept_rows)]
    ppermute x0 -> x7, waiting for transfers between devices: none -> 11.9 us  [the longest x4 9.76 us: numbers_pass(): seen_now = lax.ppermute(seen_now, axis_name='mlp', perm=kept_rows)]
    all_gather x1, waiting for transfers between devices: 92.1 us -> 99.4 us  [on_device(): lax.all_gather(w_fc_out, 'req', axis=1, tiled=True)]
  transfers between devices with their start and end apart: 10 -> 16, of which waited for: 10 -> 14; matrix products, arithmetic and copies ran while one was open for 6% -> 7% of each run, Pallas kernels for 0% -> 0%
where the time goes in v1:
time: 604 us; the launch traced here: 603 us
  waiting for transfers between devices  450 us (75%)
  blocking collectives  52.3 us (9%)
  matrix products  35.7 us (6%)
  starting transfers between devices  29.6 us (5%)
  local copies, waits for them, and re-layouts  14.1 us (2%)
  between operations  14 us (2%)
  other arithmetic  7.54 us (1%)
    all_gather x1, waiting for transfers between devices, on_device(): lax.all_gather(w_fc_out, 'req', axis=1, tiled=True)  99.4 us
    all_gather x1, waiting for transfers between devices, on_device(): lax.all_gather(w_fc_in, 'req', axis=0, tiled=True)  97.5 us
    all_gather x1, waiting for transfers between devices, on_device(): lax.all_gather(w_value, 'req', axis=0, tiled=True)  68.2 us
    all_gather x1, waiting for transfers between devices, on_device(): lax.all_gather(w_attn_out, 'req', axis=1, tiled=True)  62.7 us
    all_gather x1, waiting for transfers between devices, on_device(): lax.all_gather(w_key, 'req', axis=0, tiled=True)  42.9 us
    reduce_scatter x1, waiting for transfers between devices, on_device(): shares = lax.psum_scatter(part, 'mlp', scatter_dimension=1, tiled=True)  42.6 us
    all_to_all x1, blocking collectives, on_device(): lax.all_to_all(leaving, 'req', split_axis=0, concat_axis=0, tiled=True)  27 us
    psum x1, blocking collectives, on_device(): lax.psum((pick(down_query), pick(down_value), pick(down_fc)), 'mlp')  25.2 us
  transfers between devices with their start and end apart: 16, of which 14 were waited for; matrix products, arithmetic and copies ran while one was open for 7% of the time, Pallas kernels for 0%

profile of v1, /device:TPU:57, one launch (start us, length us, event | category | flops | bytes accessed | tf_op | source)
XLA Modules:
  0.0 603.0 jit_solution(16023295845801448230)
XLA Ops:
  6.5 0.7 all-gather.9.cloned.1.call-update
  9.9 0.9 convert_reduce_fusion.3
  11.6 0.7 all_to_all.16
  12.3 10.6 %all-to-all-start = ((bf16[32,1,2]{2,1,0:T(2,128)(2,1)}), bf16[32,1,2]{2,1,0:T(2,128)(2,1)S(1)}, u32[]{:S(2)}, u32[]{:S(2)}) async-start(bf16[32,1,2]{2,1,0:T(2,128)(2,1)} %all_to_all.16), calls=%async_computation | async-start | bytes 32768 | tf_op jit(solution)/shard_map/all_to_all | solution.py:99
  23.0 1.0 copy.46
  24.4 1.1 reshape.339
  25.6 5.1 all-to-all-done
  30.7 4.7 all-to-all-start.1
  36.7 15.6 %all-to-all-done.1 = bf16[32,2,4096]{2,1,0:T(2,128)(2,1)S(1)} async-done(((bf16[32,2,4096]{2,1,0:T(2,128)(2,1)}), bf16[32,2,4096]{2,1,0:T(2,128)(2,1)S(1)}, u32[]{:S(2)}, u32[]{:S(2)}) %all-to-all-start.1) | async-done | bytes 524320 | tf_op jit(solution)/shard_map/all_to_all | solution.py:98
  53.0 2.9 collective-permute-start
  56.1 3.0 collective-permute-done
  59.2 3.7 collective-permute-start.2
  63.7 2.5 collective-permute-done.2
  66.2 3.7 collective-permute-start.4
  69.9 0.9 collective-permute-done.3
  70.9 2.3 collective-permute-done.4
  73.2 3.7 collective-permute-start.6
  76.9 1.3 collective-permute-done.5
  78.3 1.9 collective-permute-done.6
  81.4 1.0 fusion.5
  83.1 1.4 copy-done.3
  86.2 25.2 %all-reduce = (bf16[256,16]{0,1:T(8,128)(2,1)S(1)}, bf16[256,16]{0,1:T(8,128)(2,1)S(1)}, bf16[256,16]{0,1:T(8,128)(2,1)S(1)}) all-reduce(f32[256,16]{0,1:T(8,128)S(1)} %get-tuple-element.6, f32[256,16]{0,1:T(8,128)S(1)} %get-tuple-element.7, f32[256,16]{0,1:T(8,128)S(1)} %get-tuple-element.5), channel_id=1, replica_groups=mesh['req'=32,'mlp'=8] {'mlp'}, use_global_device_ids=true, to_apply=%region_14.15 | all-reduce | flops 12288 | bytes 73728 | tf_op jit(solution)/shard_map/psum | solution.py:127
  111.5 1.0 fusion.83
  112.6 1.0 fusion.82
  113.6 0.7 fusion.84
  114.4 3.9 fusion.8
  118.2 0.9 slice.20
  119.1 0.9 slice.21
  119.9 42.9 %all-gather.11.cloned.1.call-done = bf16[4096,256]{1,0:T(8,128)(2,1)} async-done(((bf16[128,256]{1,0:T(8,128)(2,1)}), bf16[4096,256]{1,0:T(8,128)(2,1)}) %all-gather.11.cloned.1.call-update) | async-done | bytes 2097168 | tf_op jit(solution)/shard_map/all_gather | solution.py:142
  162.9 3.9 convolution_bitcast_fusion
  166.7 0.8 slice.23
  167.6 0.9 slice.24
  168.5 0.8 fusion.59
  169.4 0.9 fusion.38
  170.4 0.9 fusion.39
  171.6 0.7 copy-done.7
  172.4 68.2 %all-gather.7.cloned.1.call-done = bf16[4096,256]{1,0:T(8,128)(2,1)} async-done(((bf16[128,256]{1,0:T(8,128)(2,1)}), bf16[4096,256]{1,0:T(8,128)(2,1)}) %all-gather.7.cloned.1.call-update) | async-done | bytes 2097168 | tf_op jit(solution)/shard_map/all_gather | solution.py:143
  240.6 3.3 fusion.10
  243.9 97.5 %all-gather.15.cloned.1.call-done = bf16[4096,1024]{1,0:T(8,128)(2,1)} async-done(((bf16[128,1024]{1,0:T(8,128)(2,1)}), bf16[4096,1024]{1,0:T(8,128)(2,1)}) %all-gather.15.cloned.1.call-update) | async-done | bytes 8388624 | tf_op jit(solution)/shard_map/all_gather | solution.py:167
  341.4 99.4 %all-gather.17.cloned.1.call-done = bf16[1024,4096]{1,0:T(8,128)(2,1)} async-done(((bf16[1024,128]{1,0:T(8,128)(2,1)}), bf16[1024,4096]{1,0:T(8,128)(2,1)}) %all-gather.17.cloned.1.call-update) | async-done | bytes 8388624 | tf_op jit(solution)/shard_map/all_gather | solution.py:173
  440.8 13.1 %fusion.16 = f32[256,4096]{1,0:T(8,128)} fusion(bf16[1024,4096]{1,0:T(8,128)(2,1)} %all-gather.17.cloned.1.call-done, f32[256,1024]{1,0:T(8,128)S(1)} %fusion.84, bf16[256,4096]{1,0:T(8,128)(2,1)} %copy-done.1, bf16[4096,1024]{1,0:T(8,128)(2,1)} %all-gather.15.cloned.1.call-done, f32[1024]{0:T(1024)} %param.35), kind=kOutput, calls=%fused_computation.33 | convolution fusion | flops 4297850880 | bytes 24121344 | tf_op jit(solution)/shard_map/dot_general | solution.py:175
  453.9 62.7 %all-gather.13.cloned.1.call-done = bf16[256,4096]{1,0:T(8,128)(2,1)} async-done(((bf16[256,128]{1,0:T(8,128)(2,1)}), bf16[256,4096]{1,0:T(8,128)(2,1)}) %all-gather.13.cloned.1.call-update) | async-done | bytes 2097168 | tf_op jit(solution)/shard_map/all_gather | solution.py:172
  516.6 5.5 convolution_add_fusion
  522.1 42.6 %reduce-scatter.2.cloned.1.call-done = f32[256,512]{1,0:T(8,128)} async-done(((f32[256,4096]{1,0:T(8,128)}), f32[256,512]{1,0:T(8,128)}) %reduce-scatter.2.cloned.1.call-update) | async-done | bytes 524304 | tf_op jit(solution)/shard_map/reduce_scatter | solution.py:178
  564.7 1.1 add_convert_fusion
  566.8 27.0 %all_to_all.20 = bf16[32,2,4096]{2,1,0:T(2,128)(2,1)} all-to-all(bf16[32,2,4096]{2,1,0:T(2,128)(2,1)S(1)} %reshape.349), channel_id=1, replica_groups=mesh['req'=32,'mlp'=8] {'req'}, dimensions={0} | all-to-all | bytes 1048576 | tf_op jit(solution)/shard_map/all_to_all | solution.py:183
  593.8 1.2 reshape.350
  595.3 0.8 copy.47
  (98 shorter events, 12.1 us)
Async XLA Ops:
  6.5 107.1 %copy-start = (bf16[1024,1024]{1,0:T(8,128)(2,1)S(1)}, bf16[1024,1024]{1,0:T(8,128)(2,1)}, u32[]{:S(2)}) copy-start(bf16[1024,1024]{1,0:T(8,128)(2,1)} %param.37) | copy-start | bytes 6291460
  6.5 107.8 %all-gather.9.cloned.1.call-start = ((), (), s32[]{:S(2)}) async-start(), calls=%async_computation.5 | async-start | bytes 2162688 | tf_op jit(solution)/shard_map/all_gather | solution.py:141
  7.3 28.7 %copy-start.10 = (s32[256]{0:T(256)S(1)}, s32[256]{0:T(256)}, u32[]{:S(2)}) copy-start(s32[256]{0:T(256)} %param.22) | copy-start | bytes 3076
  7.3 28.8 %copy-start.16 = (s32[256]{0:T(256)S(1)}, s32[256]{0:T(256)}, u32[]{:S(2)}) copy-start(s32[256]{0:T(256)} %param.23) | copy-start | bytes 3076
  7.3 155.6 %all-gather.11.cloned.1.call-start = ((), (), s32[]{:S(2)}) async-start(), calls=%async_computation.6 | async-start | bytes 2162688 | tf_op jit(solution)/shard_map/all_gather | solution.py:142
  8.0 232.6 %all-gather.7.cloned.1.call-start = ((), (), s32[]{:S(2)}) async-start(), calls=%async_computation.4 | async-start | bytes 2162688 | tf_op jit(solution)/shard_map/all_gather | solution.py:143
  8.8 332.6 %all-gather.15.cloned.1.call-start = ((), (), s32[]{:S(2)}) async-start(), calls=%async_computation.8 | async-start | bytes 8650752 | tf_op jit(solution)/shard_map/all_gather | solution.py:167
  9.3 431.5 %all-gather.17.cloned.1.call-start = ((), (), s32[]{:S(2)}) async-start(), calls=%async_computation.9 | async-start | bytes 8650752 | tf_op jit(solution)/shard_map/all_gather | solution.py:173
  11.5 25.2 %copy-start.12 = (s32[32]{0:T(128)}, s32[32]{0:T(128)S(1)}, u32[]{:S(2)}) copy-start(s32[32]{0:T(128)S(1)} %multiply_add_fusion.1) | copy-start | bytes 388
  12.3 18.4 %all-to-all-start = ((bf16[32,1,2]{2,1,0:T(2,128)(2,1)}), bf16[32,1,2]{2,1,0:T(2,128)(2,1)S(1)}, u32[]{:S(2)}, u32[]{:S(2)}) async-start(bf16[32,1,2]{2,1,0:T(2,128)(2,1)} %all_to_all.16), calls=%async_computation | async-start | bytes 32768 | tf_op jit(solution)/shard_map/all_to_all | solution.py:99
  30.7 21.7 %all-to-all-start.1 = ((bf16[32,2,4096]{2,1,0:T(2,128)(2,1)}), bf16[32,2,4096]{2,1,0:T(2,128)(2,1)S(1)}, u32[]{:S(2)}, u32[]{:S(2)}) async-start(bf16[32,2,4096]{2,1,0:T(2,128)(2,1)} %reshape.339), calls=%async_computation.1 | async-start | bytes 1048576 | tf_op jit(solution)/shard_map/all_to_all | solution.py:98
  35.3 481.3 %all-gather.13.cloned.1.call-start = ((), (), s32[]{:S(2)}) async-start(), calls=%async_computation.7 | async-start | bytes 2162688 | tf_op jit(solution)/shard_map/all_gather | solution.py:172
  35.9 528.8 %reduce-scatter.2.cloned.1.call-start = ((), (), s32[]{:S(2)}) async-start(), calls=%async_computation.10 | async-start | bytes 4718592 | tf_op jit(solution)/shard_map/reduce_scatter | solution.py:178
  36.0 19.9 %copy-start.14 = (f32[32]{0:T(128)}, f32[32]{0:T(128)S(1)}, u32[]{:S(2)}) copy-start(f32[32]{0:T(128)S(1)} %iota_convert_fusion) | copy-start | bytes 388
  53.0 6.2 %collective-permute-start = (bf16[256,512]{1,0:T(8,128)(2,1)S(1)}, bf16[256,512]{1,0:T(8,128)(2,1)S(1)}, u32[]{:S(2)}, u32[]{:S(2)}) collective-permute-start(bf16[256,512]{1,0:T(8,128)(2,1)S(1)} %reshape.341), channel_id=1, source_target_pairs={{0,1},{1,2},{2,3},{3,4},{4,5},{5,6},{6,7},{7,0},{8,9},{9,10},{10,1... | collective-permute-start | bytes 786440 | tf_op jit(solution)/shard_map/ppermute | solution.py:25
  56.0 7.4 %collective-permute-start.1 = (bf16[256,512]{1,0:T(8,128)(2,1)S(1)}, bf16[256,512]{1,0:T(8,128)(2,1)S(1)}, u32[]{:S(2)}, u32[]{:S(2)}) collective-permute-start(bf16[256,512]{1,0:T(8,128)(2,1)S(1)} %reshape.341), channel_id=1, source_target_pairs={{0,7},{1,0},{2,1},{3,2},{4,3},{5,4},{6,5},{7,6},{8,15},{9,8},{10,9... | collective-permute-start | bytes 786440 | tf_op jit(solution)/shard_map/ppermute | solution.py:30
  59.2 7.0 %collective-permute-start.2 = (bf16[256,512]{1,0:T(8,128)(2,1)S(1)}, bf16[256,512]{1,0:T(8,128)(2,1)S(1)}, u32[]{:S(2)}, u32[]{:S(2)}) collective-permute-start(bf16[256,512]{1,0:T(8,128)(2,1)S(1)} %collective-permute-done), channel_id=1, source_target_pairs={{0,1},{1,2},{2,3},{3,4},{4,5},{5,6},{6,7},{7,0},{8,9},{9,10},{10,1... | collective-permute-start | bytes 786440 | tf_op jit(solution)/shard_map/ppermute | solution.py:25
  63.4 7.4 %collective-permute-start.3 = (bf16[256,512]{1,0:T(8,128)(2,1)S(1)}, bf16[256,512]{1,0:T(8,128)(2,1)S(1)}, u32[]{:S(2)}, u32[]{:S(2)}) collective-permute-start(bf16[256,512]{1,0:T(8,128)(2,1)S(1)} %collective-permute-done.1), channel_id=1, source_target_pairs={{0,7},{1,0},{2,1},{3,2},{4,3},{5,4},{6,5},{7,6},{8,15},{9,8},{10,9... | collective-permute-start | bytes 786440 | tf_op jit(solution)/shard_map/ppermute | solution.py:30
  66.2 7.0 %collective-permute-start.4 = (bf16[256,512]{1,0:T(8,128)(2,1)S(1)}, bf16[256,512]{1,0:T(8,128)(2,1)S(1)}, u32[]{:S(2)}, u32[]{:S(2)}) collective-permute-start(bf16[256,512]{1,0:T(8,128)(2,1)S(1)} %collective-permute-done.2), channel_id=1, source_target_pairs={{0,1},{1,2},{2,3},{3,4},{4,5},{5,6},{6,7},{7,0},{8,9},{9,10},{10,1... | collective-permute-start | bytes 786440 | tf_op jit(solution)/shard_map/ppermute | solution.py:25
  70.8 7.4 %collective-permute-start.5 = (bf16[256,512]{1,0:T(8,128)(2,1)S(1)}, bf16[256,512]{1,0:T(8,128)(2,1)S(1)}, u32[]{:S(2)}, u32[]{:S(2)}) collective-permute-start(bf16[256,512]{1,0:T(8,128)(2,1)S(1)} %collective-permute-done.3), channel_id=1, source_target_pairs={{0,7},{1,0},{2,1},{3,2},{4,3},{5,4},{6,5},{7,6},{8,15},{9,8},{10,9... | collective-permute-start | bytes 786440 | tf_op jit(solution)/shard_map/ppermute | solution.py:30
  73.2 7.0 %collective-permute-start.6 = (bf16[256,512]{1,0:T(8,128)(2,1)S(1)}, bf16[256,512]{1,0:T(8,128)(2,1)S(1)}, u32[]{:S(2)}, u32[]{:S(2)}) collective-permute-start(bf16[256,512]{1,0:T(8,128)(2,1)S(1)} %collective-permute-done.4), channel_id=1, source_target_pairs={{0,1},{1,2},{2,3},{3,4},{4,5},{5,6},{6,7},{7,0},{8,9},{9,10},{10,1... | collective-permute-start | bytes 786440 | tf_op jit(solution)/shard_map/ppermute | solution.py:25
  80.2 1.1 copy-start.8
  80.2 1.1 copy-start.9
  81.3 1.2 copy-start.2
  82.6 2.6 copy-start.1
  82.6 2.0 copy-start.3
  82.6 2.6 copy-start.4
  85.7 25.8 %copy-start.5 = (bf16[1024,256]{1,0:T(8,128)(2,1)S(1)}, bf16[1024,256]{1,0:T(8,128)(2,1)}, u32[]{:S(2)}) copy-start(bf16[1024,256]{1,0:T(8,128)(2,1)} %param.31) | copy-start | bytes 1572868
  86.2 26.4 %copy-start.6 = (bf16[1024,256]{1,0:T(8,128)(2,1)S(1)}, bf16[1024,256]{1,0:T(8,128)(2,1)}, u32[]{:S(2)}) copy-start(bf16[1024,256]{1,0:T(8,128)(2,1)} %param.33) | copy-start | bytes 1572868
  171.6 0.7 copy-start.7
  522.1 42.6 %copy-start.11 = (f32[512]{0:T(512)S(1)}, f32[512]{0:T(512)}, u32[]{:S(2)}) copy-start(f32[512]{0:T(512)} %param.39) | copy-start | bytes 6148
  522.1 43.9 %copy-start.15 = (f32[32]{0:T(128)S(1)}, f32[32]{0:T(128)}, u32[]{:S(2)}) copy-start(f32[32]{0:T(128)} %copy-done.14) | copy-start | bytes 388
  566.0 29.1 %copy-start.13 = (s32[32]{0:T(128)S(1)}, s32[32]{0:T(128)}, u32[]{:S(2)}) copy-start(s32[32]{0:T(128)} %copy-done.12) | copy-start | bytes 388
Sparse Core Ops, SparseCore 0:
  9.9 75.1 all-gather.8
  87.7 75.0 all-gather.10
  165.5 75.0 all-gather.6
  243.1 98.2 all-gather.14
  343.7 97.0 all-gather.16
  443.1 73.4 all-gather.12
  522.3 42.4 reduce-scatter.1
